TPU v7x, 128 devices: a whole 4x4x4 slice. The times are simulated.
128 devices in a mesh: req: 16 (over x, y), vocab: 8 (over z, core).
Axes of the slice: x: 4, y: 4, z: 4, core: 2. Of those that a mesh axis runs over, the one named last changes fastest.
Arguments:
- hidden: bfloat16 [64, 128, 2048], P('req'), may hold values from -1000 to 1000
- gain: float32 [2048], replicated, may hold values from 0.5 to 1.5
- embedding: bfloat16 [76800, 2048], P('vocab', 'req'), may hold values from -16 to 16
- targets: int32 [64, 128], P('req'), may hold values from 0 to 76799
- span_start: int32 [64], P('req'), may hold values from 0 to 127, as said below
- span_len: int32 [64], P('req'), may hold values from 1 to 128
- deal_order: int32 [64], replicated, may hold values from 0 to 63, as said below
Outputs:
- logprob: float32 [64, 128], P('req')
- entropy: float32 [64, 128], P('req')
Inputs may be any that keep to these rules, and one draw needn't show every extreme that they name: deal_order is a permutation of the requests; the span lengths of the 4 requests dealt to one group add up to at most 224, exactly 224 for some group. span_start + span_len <= 128 for every request.
All inputs are finite; a program needn't handle non-finite values.
Results may differ from a plain program's by a relative error of at most 0.0029.
Values may be sent and summed in bfloat16 or wider, within the bound.
No kernel may reach another device: no remote copies, remote signals or barrier semaphores. Data moves between devices by JAX's collectives and lax.ppermute only.
A program may use at most 128 MiB of HBM per device.

v0:
```python
import jax
import jax.numpy as jnp
from jax import lax
from jax.sharding import PartitionSpec as P

CAP = 224
eps = 1e-06


def compact_plan(row_base, lengths, capacity):
    offsets = jnp.cumsum(lengths) - lengths
    counter = jnp.arange(capacity, dtype=jnp.int32)
    member = jnp.sum((counter[:, None] >= offsets[None, :]).astype(jnp.int32), axis=1) - 1
    member_hot = (member[:, None] == jnp.arange(lengths.shape[0], dtype=jnp.int32)[None, :]).astype(
        jnp.int32
    )
    row_index = jnp.sum(member_hot * (row_base - offsets)[None, :], axis=1) + counter
    in_span = counter < jnp.sum(lengths)
    return (row_index, in_span)


def normalize(rows, gain):
    wide_rows = rows.astype(jnp.float32)
    scale = lax.rsqrt(jnp.mean(wide_rows * wide_rows, axis=1, keepdims=True) + eps)
    return (wide_rows * scale * gain).astype(jnp.bfloat16)


def shards(hidden, gain, embedding, targets, span_start, span_len, deal_order):
    per_dev = hidden.shape[0]
    slot_len = hidden.shape[1]
    width = hidden.shape[2]
    total = deal_order.shape[0]
    voc_local = embedding.shape[0]
    here = lax.axis_index("req")
    positions = jnp.arange(total, dtype=jnp.int32)
    source_of = jnp.sum(
        jnp.where(deal_order[None, :] == positions[:, None], positions[None, :], 0), axis=1
    )
    all_starts, all_lengths = (
        lax.all_gather(span_start, "req", axis=0, tiled=True),
        lax.all_gather(span_len, "req", axis=0, tiled=True),
    )
    my_slots = here * per_dev + jnp.arange(per_dev, dtype=jnp.int32)
    members = jnp.sum(
        jnp.where(my_slots[:, None] == positions[None, :], source_of[None, :], 0), axis=1
    )
    member_hot = members[:, None] == positions[None, :]
    lengths = jnp.sum(jnp.where(member_hot, all_lengths[None, :], 0), axis=1)
    starts = jnp.sum(jnp.where(member_hot, all_starts[None, :], 0), axis=1)
    row_base = jnp.arange(per_dev, dtype=jnp.int32) * slot_len + starts
    row_index, in_span = compact_plan(row_base, lengths, CAP)
    safe_index = jnp.where(in_span, row_index, 0)
    spread_rows, spread_marks = (
        lax.all_to_all(hidden, "req", split_axis=1, concat_axis=0, tiled=True),
        lax.all_to_all(targets, "req", split_axis=1, concat_axis=0, tiled=True),
    )
    dealt_rows = jnp.take(spread_rows, source_of, axis=0)
    dealt_marks = jnp.take(spread_marks, source_of, axis=0)
    home_rows, home_marks = (
        lax.all_to_all(dealt_rows, "req", split_axis=0, concat_axis=1, tiled=True),
        lax.all_to_all(dealt_marks, "req", split_axis=0, concat_axis=1, tiled=True),
    )
    rows = jnp.take(home_rows.reshape(per_dev * slot_len, width), safe_index, axis=0)
    target_ids = jnp.where(
        in_span, jnp.take(home_marks.reshape(per_dev * slot_len), safe_index), -1
    )
    normed = normalize(rows, gain)
    logits = lax.dot_general(
        normed,
        lax.all_gather(embedding, "req", axis=1, tiled=True),
        (((1,), (1,)), ((), ())),
        preferred_element_type=jnp.float32,
    )
    local_top = jnp.max(logits, axis=1)
    shifted = logits - local_top[:, None]
    weights = jnp.exp(shifted)
    local_mass = jnp.sum(weights, axis=1)
    local_spread = jnp.sum(weights * shifted, axis=1)
    local_ids = target_ids - lax.axis_index("vocab") * voc_local
    local_target = jnp.sum(
        jnp.where(
            jnp.arange(voc_local, dtype=jnp.int32)[None, :] == local_ids[:, None], logits, 0.0
        ),
        axis=1,
    )
    row_top = lax.pmax(local_top, "vocab")
    factor = jnp.exp(local_top - row_top)
    row_mass, row_spread, row_target = lax.psum(
        (
            factor * local_mass,
            factor * (local_spread + (local_top - row_top) * local_mass),
            local_target,
        ),
        "vocab",
    )
    log_mass = jnp.log(row_mass)
    compact_logprob = jnp.where(in_span, row_target - row_top - log_mass, 0.0)
    compact_entropy = jnp.where(in_span, log_mass - row_spread / row_mass, 0.0)
    spot = jnp.where(in_span, row_index, per_dev * slot_len)
    dealt_logprob = (
        jnp.zeros((per_dev * slot_len,), jnp.float32)
        .at[spot]
        .set(compact_logprob, mode="drop")
        .reshape(per_dev, slot_len)
    )
    dealt_entropy = (
        jnp.zeros((per_dev * slot_len,), jnp.float32)
        .at[spot]
        .set(compact_entropy, mode="drop")
        .reshape(per_dev, slot_len)
    )
    wide_logprob, wide_entropy = (
        lax.all_to_all(dealt_logprob, "req", split_axis=1, concat_axis=0, tiled=True),
        lax.all_to_all(dealt_entropy, "req", split_axis=1, concat_axis=0, tiled=True),
    )
    home_logprob = jnp.take(wide_logprob, deal_order, axis=0)
    home_entropy = jnp.take(wide_entropy, deal_order, axis=0)
    out_logprob, out_entropy = (
        lax.all_to_all(home_logprob, "req", split_axis=0, concat_axis=1, tiled=True),
        lax.all_to_all(home_entropy, "req", split_axis=0, concat_axis=1, tiled=True),
    )
    return (out_logprob, out_entropy)


def solution(mesh):
    in_specs = (
        P("req", None, None),
        P(),
        P("vocab", "req"),
        P("req", None),
        P("req"),
        P("req"),
        P(),
    )
    out_specs = (P("req", None), P("req", None))
    return jax.shard_map(shards, mesh=mesh, in_specs=in_specs, out_specs=out_specs, check_vma=False)
```

profile of v0, /device:TPU:0, one launch (start us, length us, event | category | flops | bytes accessed | tf_op | source)
XLA Modules:
  0.0 401.7 jit_solution(16751751695467223779)
XLA Ops:
  8.6 7.1 %all-to-all-start = ((s32[4,16,8]{2,0,1:T(4,128)}), s32[4,16,8]{2,0,1:T(4,128)S(1)}, u32[]{:S(2)}, u32[]{:S(2)}) async-start(s32[4,16,8]{2,0,1:T(4,128)} %copy.39), calls=%async_computation | async-start | bytes 65536 | tf_op jit(solution)/shard_map/all_to_all | solution.py:55
  15.8 2.9 copy.41
  18.7 4.7 %all-to-all-done = s32[4,16,8]{2,0,1:T(4,128)S(1)} async-done(((s32[4,16,8]{2,0,1:T(4,128)}), s32[4,16,8]{2,0,1:T(4,128)S(1)}, u32[]{:S(2)}, u32[]{:S(2)}) %all-to-all-start) | async-done | bytes 2080 | tf_op jit(solution)/shard_map/all_to_all | solution.py:55
  23.4 3.7 all-to-all-start.2
  28.7 39.2 %all-to-all-done.2 = bf16[4,128,2048]{2,0,1:T(4,128)(2,1)S(1)} async-done(((bf16[4,128,2048]{2,0,1:T(4,128)(2,1)}), bf16[4,128,2048]{2,0,1:T(4,128)(2,1)S(1)}, u32[]{:S(2)}, u32[]{:S(2)}) %all-to-all-start.2) | async-done | bytes 2097184 | tf_op jit(solution)/shard_map/all_to_all | solution.py:54
  67.9 4.7 %all-to-all-start.1 = ((s32[16,4,8]{2,1,0:T(4,128)}), s32[16,4,8]{2,1,0:T(4,128)S(1)}, u32[]{:S(2)}, u32[]{:S(2)}) async-start(s32[16,4,8]{2,1,0:T(4,128)} %broadcast_select_fusion.5), calls=%async_computation.1 | async-start | bytes 65536 | tf_op jit(solution)/shard_map/all_to_all | solution.py:61
  72.6 1.2 copy.50
  73.8 1.4 copy.43
  75.2 2.3 gather_fusion.2
  77.5 1.6 broadcast_select_fusion
  79.1 1.3 all-to-all-done.1
  80.4 6.1 %all-to-all-start.3 = ((bf16[64,8,2048]{2,1,0:T(8,128)(2,1)}), bf16[64,8,2048]{2,1,0:T(8,128)(2,1)S(1)}, u32[]{:S(2)}, u32[]{:S(2)}) async-start(bf16[64,8,2048]{2,1,0:T(8,128)(2,1)} %broadcast_select_fusion), calls=%async_computation.3 | async-start | bytes 4194304 | tf_op jit(solution)/shard_map/all_to_all | solution.py:60
  88.2 37.1 %all-reduce.2 = (s32[64]{0:T(128)S(1)}, s32[64]{0:T(128)S(1)}) all-reduce(s32[64]{0:T(128)S(1)} %dynamic-update-slice, s32[64]{0:T(128)S(1)} %dynamic-update-slice.1), channel_id=1, replica_groups=mesh['req'=16,'vocab'=8] {'req'}, use_global_device_ids=true, to_apply=%add | all-reduce | flops 128 | bytes 1024
  125.5 0.7 select_reduce_fusion.4
  127.4 1.9 gather_fusion.1
  130.0 1.3 copy-done
  131.3 1.8 copy.44
  133.1 1.3 gather_fusion.3
  134.8 157.2 %all-gather.2.cloned.1.call-done = bf16[9600,2048]{1,0:T(8,128)(2,1)} async-done(((bf16[9600,128]{1,0:T(8,128)(2,1)}), bf16[9600,2048]{1,0:T(8,128)(2,1)}) %all-gather.2.cloned.1.call-update) | async-done | bytes 39321616 | tf_op jit(solution)/shard_map/all_gather | solution.py:70
  291.9 21.5 %fusion.14 = (f32[224]{0:T(256)S(1)}, f32[224,9600]{1,0:T(8,128)}) fusion(bf16[9600,2048]{1,0:T(8,128)(2,1)} %all-gather.2.cloned.1.call-done, f32[2048]{0:T(1024)S(1)} %copy-done.3, f32[224]{0:T(256)S(1)} %add_rsqrt_fusion, bf16[224,2048]{1,0:T(8,128)(2,1)S(1)} %gather_fusion.3, pred[224]{0:T(512)(128)(4,1)S(1)} %get-tuple-element.15), kind=kOutput, calls=%fused_computation.73 | convolution fusion | flops 8812482560 | bytes 48850912 | tf_op jit(solution)/shard_map/dot_general | solution.py:68
  313.5 13.6 %pmax.7 = f32[224]{0:T(256)S(1)} all-reduce(f32[224]{0:T(256)S(1)} %get-tuple-element.26), channel_id=1, replica_groups=mesh['req'=16,'vocab'=8] {'vocab'}, use_global_device_ids=true, to_apply=%region_12.13 | all-reduce | flops 224 | bytes 1792 | tf_op jit(solution)/shard_map/pmax | solution.py:86
  327.1 5.3 %fusion = (f32[224]{0:T(256)S(1)}, f32[224]{0:T(256)S(1)}, f32[224]{0:T(256)S(1)}) fusion(f32[224,9600]{1,0:T(8,128)} %get-tuple-element.27, f32[224]{0:T(256)S(1)} %get-tuple-element.26, s32[224]{0:T(256)S(1)} %get-tuple-element.14), kind=kLoop, calls=%fused_computation.10 | loop fusion | flops 15052128 | bytes 8606080 | tf_op jit(solution)/shard_map/reduce_sum | solution.py:78
  332.4 12.4 %all-reduce.3 = (f32[224]{0:T(256)S(1)}, f32[224]{0:T(256)S(1)}, f32[224]{0:T(256)S(1)}) all-reduce(f32[224]{0:T(256)S(1)} %get-tuple-element.5, f32[224]{0:T(256)S(1)} %get-tuple-element.19, f32[224]{0:T(256)S(1)} %get-tuple-element.18), channel_id=1, replica_groups=mesh['req'=16,'vocab'=8] {'vocab'}, use_global_device_ids=true, to_apply=%region_10.11 | all-reduce | flops 672 | bytes 5376 | tf_op jit(solution)/shard_map/psum | solution.py:88
  345.5 1.3 scatter_custom_fusion.1
  347.5 4.9 %all-to-all-start.6 = ((f32[4,16,8]{2,0,1:T(4,128)}), f32[4,16,8]{2,0,1:T(4,128)S(1)}, u32[]{:S(2)}, u32[]{:S(2)}) async-start(f32[4,16,8]{2,0,1:T(4,128)} %copy.47), calls=%async_computation.6 | async-start | bytes 65536 | tf_op jit(solution)/shard_map/all_to_all | solution.py:114
  352.4 1.3 scatter_custom_fusion
  354.5 5.6 %all-to-all-done.6 = f32[4,16,8]{2,0,1:T(4,128)S(1)} async-done(((f32[4,16,8]{2,0,1:T(4,128)}), f32[4,16,8]{2,0,1:T(4,128)S(1)}, u32[]{:S(2)}, u32[]{:S(2)}) %all-to-all-start.6) | async-done | bytes 2080 | tf_op jit(solution)/shard_map/all_to_all | solution.py:114
  360.0 3.5 all-to-all-start.4
  364.1 6.9 %all-to-all-done.4 = f32[4,16,8]{2,0,1:T(4,128)S(1)} async-done(((f32[4,16,8]{2,0,1:T(4,128)}), f32[4,16,8]{2,0,1:T(4,128)S(1)}, u32[]{:S(2)}, u32[]{:S(2)}) %all-to-all-start.4) | async-done | bytes 2080 | tf_op jit(solution)/shard_map/all_to_all | solution.py:113
  372.4 10.7 %all_to_all.141 = f32[16,4,8]{2,1,0:T(4,128)S(1)} all-to-all(f32[16,4,8]{2,1,0:T(4,128)S(1)} %bitcast.49), channel_id=1, replica_groups=mesh['req'=16,'vocab'=8] {'req'}, dimensions={0} | all-to-all | bytes 4096 | tf_op jit(solution)/shard_map/all_to_all | solution.py:119
  383.1 3.5 all-to-all-start.7
  387.3 6.9 %all-to-all-done.7 = f32[16,4,8]{2,1,0:T(4,128)S(1)} async-done(((f32[16,4,8]{2,1,0:T(4,128)}), f32[16,4,8]{2,1,0:T(4,128)S(1)}, u32[]{:S(2)}, u32[]{:S(2)}) %all-to-all-start.7) | async-done | bytes 2080 | tf_op jit(solution)/shard_map/all_to_all | solution.py:120
  (63 shorter events, 11.7 us)
Async XLA Ops:
  7.2 0.8 copy-start.2
  7.2 8.6 %copy-start.1 = (bf16[4,128,2048]{2,1,0:T(8,128)(2,1)S(1)}, bf16[4,128,2048]{2,1,0:T(8,128)(2,1)}, u32[]{:S(2)}) copy-start(bf16[4,128,2048]{2,1,0:T(8,128)(2,1)} %param.9) | copy-start | bytes 6291460
  7.2 284.8 %all-gather.2.cloned.1.call-start = ((), (), s32[]{:S(2)}) async-start(), calls=%async_computation.8 | async-start | bytes 41779200 | tf_op jit(solution)/shard_map/all_gather | solution.py:70
  8.6 14.8 %all-to-all-start = ((s32[4,16,8]{2,0,1:T(4,128)}), s32[4,16,8]{2,0,1:T(4,128)S(1)}, u32[]{:S(2)}, u32[]{:S(2)}) async-start(s32[4,16,8]{2,0,1:T(4,128)} %copy.39), calls=%async_computation | async-start | bytes 65536 | tf_op jit(solution)/shard_map/all_to_all | solution.py:55
  18.7 8.4 %copy-start.6 = (s32[64]{0:T(128)S(1)}, s32[64]{0:T(128)}, u32[]{:S(2)}) copy-start(s32[64]{0:T(128)} %param.15) | copy-start | bytes 772
  23.4 44.5 %all-to-all-start.2 = ((bf16[4,128,2048]{2,0,1:T(4,128)(2,1)}), bf16[4,128,2048]{2,0,1:T(4,128)(2,1)S(1)}, u32[]{:S(2)}, u32[]{:S(2)}) async-start(bf16[4,128,2048]{2,0,1:T(4,128)(2,1)} %copy.41), calls=%async_computation.2 | async-start | bytes 4194304 | tf_op jit(solution)/shard_map/all_to_all | solution.py:54
  67.9 12.5 %all-to-all-start.1 = ((s32[16,4,8]{2,1,0:T(4,128)}), s32[16,4,8]{2,1,0:T(4,128)S(1)}, u32[]{:S(2)}, u32[]{:S(2)}) async-start(s32[16,4,8]{2,1,0:T(4,128)} %broadcast_select_fusion.5), calls=%async_computation.1 | async-start | bytes 65536 | tf_op jit(solution)/shard_map/all_to_all | solution.py:61
  79.1 7.4 %copy-start.7 = (u32[128]{0:T(128)S(1)}, u32[128]{0:T(128)}, u32[]{:S(2)}) copy-start(u32[128]{0:T(128)} %constant.108) | copy-start | bytes 1540
  79.1 8.7 %copy-start.4 = (s32[4]{0:T(128)S(1)}, s32[4]{0:T(128)}, u32[]{:S(2)}) copy-start(s32[4]{0:T(128)} %param.14) | copy-start | bytes 52
  79.1 8.9 %copy-start.5 = (s32[4]{0:T(128)S(1)}, s32[4]{0:T(128)}, u32[]{:S(2)}) copy-start(s32[4]{0:T(128)} %param.13) | copy-start | bytes 52
  80.4 49.6 %all-to-all-start.3 = ((bf16[64,8,2048]{2,1,0:T(8,128)(2,1)}), bf16[64,8,2048]{2,1,0:T(8,128)(2,1)S(1)}, u32[]{:S(2)}, u32[]{:S(2)}) async-start(bf16[64,8,2048]{2,1,0:T(8,128)(2,1)} %broadcast_select_fusion), calls=%async_computation.3 | async-start | bytes 4194304 | tf_op jit(solution)/shard_map/all_to_all | solution.py:60
  130.0 1.3 copy-start
  133.1 158.8 %copy-start.3 = (f32[2048]{0:T(1024)S(1)}, f32[2048]{0:T(1024)}, u32[]{:S(2)}) copy-start(f32[2048]{0:T(1024)} %param.10) | copy-start | bytes 24580
  347.5 12.6 %all-to-all-start.6 = ((f32[4,16,8]{2,0,1:T(4,128)}), f32[4,16,8]{2,0,1:T(4,128)S(1)}, u32[]{:S(2)}, u32[]{:S(2)}) async-start(f32[4,16,8]{2,0,1:T(4,128)} %copy.47), calls=%async_computation.6 | async-start | bytes 65536 | tf_op jit(solution)/shard_map/all_to_all | solution.py:114
  360.0 11.0 %all-to-all-start.4 = ((f32[4,16,8]{2,0,1:T(4,128)}), f32[4,16,8]{2,0,1:T(4,128)S(1)}, u32[]{:S(2)}, u32[]{:S(2)}) async-start(f32[4,16,8]{2,0,1:T(4,128)} %copy.45), calls=%async_computation.4 | async-start | bytes 65536 | tf_op jit(solution)/shard_map/all_to_all | solution.py:113
  383.1 11.1 %all-to-all-start.7 = ((f32[16,4,8]{2,1,0:T(4,128)}), f32[16,4,8]{2,1,0:T(4,128)S(1)}, u32[]{:S(2)}, u32[]{:S(2)}) async-start(f32[16,4,8]{2,1,0:T(4,128)} %bitcast.24), calls=%async_computation.7 | async-start | bytes 65536 | tf_op jit(solution)/shard_map/all_to_all | solution.py:120
Sparse Core Ops, SparseCore 0:
  10.1 281.7 all-gather.1
where the time goes:
time: 402 us
  waiting for transfers between devices  222 us (55%)
  blocking collectives  73.8 us (18%)
  starting transfers between devices  33.6 us (8%)
  local copies, waits for them, and re-layouts  23.2 us (6%)
  matrix products  21.5 us (5%)
  between operations  15 us (4%)
  other arithmetic  12 us (3%)
    all_gather x1, waiting for transfers between devices, shards(): lax.all_gather(embedding, 'req', axis=1, tiled=True)  157 us
    all_to_all x1, waiting for transfers between devices, shards(): lax.all_to_all(hidden, 'req', split_axis=1, concat_axis=0, tiled=True)  39.2 us
    unnamed x1, blocking collectives  37.1 us
    dot_general x1, matrix products, shards(): lax.dot_general(normed, lax.all_gather(embedding, 'req', axis=1, tiled=Tr...  21.5 us
    pmax x1, blocking collectives, shards(): row_top = lax.pmax(local_top, 'vocab')  13.6 us
    psum x1, blocking collectives, shards(): lax.psum((factor * local_mass, factor * (local_spread + (local_top - row_...  12.4 us
    all_to_all x1, blocking collectives, shards(): lax.all_to_all(home_logprob, 'req', split_axis=0, concat_axis=1, tiled=True)  10.7 us
  transfers between devices with their start and end apart: 8, of which 7 were waited for; matrix products, arithmetic and copies ran while one was open for 6% of the time, Pallas kernels for 0%

commit v1 on v0

--- a/solution.py
+++ b/solution.py
@@ -5,6 +5,14 @@
 
 CAP = 224
 eps = 1e-06
+
+
+def gather_by_exchange(value, axis, dim):
+    size = lax.axis_size(axis)
+    repeats = [size if d == dim else 1 for d in range(value.ndim)]
+    return lax.all_to_all(
+        jnp.tile(value, repeats), axis, split_axis=dim, concat_axis=dim, tiled=True
+    )
 
 
 def compact_plan(row_base, lengths, capacity):
@@ -67,7 +75,7 @@
     normed = normalize(rows, gain)
     logits = lax.dot_general(
         normed,
-        lax.all_gather(embedding, "req", axis=1, tiled=True),
+        gather_by_exchange(embedding, "req", 1),
         (((1,), (1,)), ((), ())),
         preferred_element_type=jnp.float32,
     )

time: 402 us -> 982 us (2.44)
  blocking collectives: 73.8 us -> 774 us
  waiting for transfers between devices: 222 us -> 52.7 us
  local copies, waits for them, and re-layouts: 23.2 us -> 81.3 us
  between operations: 15 us -> 1.61 us
    unnamed x1, blocking collectives: 37.1 us -> 708 us
    all_gather x1 -> x0, waiting for transfers between devices: 157 us -> none  [shards(): lax.all_gather(embedding, 'req', axis=1, tiled=True)]
    all_to_all x0 -> x1, local copies, waits for them, and re-layouts: none -> 45.7 us  [gather_by_exchange(): lax.all_to_all(jnp.tile(value, repeats), axis, split_axis=dim, concat_axi...]
    all_to_all x0 -> x1, blocking collectives: none -> 30.1 us  [shards(): lax.all_to_all(dealt_rows, 'req', split_axis=0, concat_axis=1, tiled=True)]
    another operation x0 -> x1, local copies, waits for them, and re-layouts: none -> 13 us  [gather_by_exchange(): jnp.tile(value, repeats)]
    all_to_all x1, waiting for transfers between devices: 39.2 us -> 27.8 us  [shards(): lax.all_to_all(hidden, 'req', split_axis=1, concat_axis=0, tiled=True)]
  transfers between devices with their start and end apart: 8 -> 7, of which waited for: 7 -> 6; matrix products, arithmetic and copies ran while one was open for 6% -> 2% of each run, Pallas kernels for 0% -> 0%
where the time goes in v1:
time: 982 us; the launch traced here: 980 us
  blocking collectives  774 us (79%)
  local copies, waits for them, and re-layouts  81.3 us (8%)
  waiting for transfers between devices  52.7 us (5%)
  starting transfers between devices  38.5 us (4%)
  matrix products  19.4 us (2%)
  other arithmetic  12.3 us (1%)
    unnamed x1, blocking collectives  708 us
    all_to_all x1, local copies, waits for them, and re-layouts, gather_by_exchange(): lax.all_to_all(jnp.tile(value, repeats), axis, split_axis=dim, concat_axi...  45.7 us
    all_to_all x1, blocking collectives, shards(): lax.all_to_all(dealt_rows, 'req', split_axis=0, concat_axis=1, tiled=True)  30.1 us
    all_to_all x1, waiting for transfers between devices, shards(): lax.all_to_all(hidden, 'req', split_axis=1, concat_axis=0, tiled=True)  27.8 us
  transfers between devices with their start and end apart: 7, of which 6 were waited for; matrix products, arithmetic and copies ran while one was open for 2% of the time, Pallas kernels for 0%

profile of v1, /device:TPU:0, one launch (start us, length us, event | category | flops | bytes accessed | tf_op | source)
XLA Modules:
  0.0 980.2 jit_solution(1546213186532935723)
XLA Ops:
  0.6 0.8 all_to_all.110
  2.0 7.1 all-to-all-start
  9.2 4.6 copy.52
  13.7 3.1 all-to-all-done
  16.8 4.3 all-to-all-start.2
  22.6 27.8 %all-to-all-done.2 = bf16[4,128,2048]{2,0,1:T(4,128)(2,1)S(1)} async-done(((bf16[4,128,2048]{2,0,1:T(4,128)(2,1)}), bf16[4,128,2048]{2,0,1:T(4,128)(2,1)S(1)}, u32[]{:S(2)}, u32[]{:S(2)}) %all-to-all-start.2) | async-done | bytes 2097184 | tf_op jit(solution)/shard_map/all_to_all | solution.py:62
  50.4 4.0 all-to-all-start.1
  54.4 1.2 copy.62
  55.7 2.0 gather_fusion.2
  57.7 1.8 broadcast_select_fusion
  59.6 2.4 all-to-all-done.1
  62.0 30.1 %all_to_all.150 = bf16[64,8,2048]{2,1,0:T(8,128)(2,1)} all-to-all(bf16[64,8,2048]{2,1,0:T(8,128)(2,1)S(1)} %broadcast_select_fusion), channel_id=1, replica_groups=mesh['req'=16,'vocab'=8] {'req'}, dimensions={0} | all-to-all | bytes 4194304 | tf_op jit(solution)/shard_map/all_to_all | solution.py:68
  92.1 13.0 %tile.2 = bf16[9600,16,128]{2,0,1:T(8,128)(2,1)} broadcast(bf16[9600,128]{1,0:T(8,128)(2,1)S(1)} %copy-done), dimensions={0,2} | broadcast | bytes 41779200 | tf_op jit(solution)/shard_map/tile | solution.py:14
  105.1 6.3 all-to-all-start.4
  113.2 707.7 %all-reduce.2 = (s32[64]{0:T(128)S(1)}, s32[64]{0:T(128)S(1)}) all-reduce(s32[64]{0:T(128)S(1)} %dynamic-update-slice, s32[64]{0:T(128)S(1)} %dynamic-update-slice.1), channel_id=1, replica_groups=mesh['req'=16,'vocab'=8] {'req'}, use_global_device_ids=true, to_apply=%add | all-reduce | flops 128 | bytes 1024
  822.9 1.9 gather_fusion.1
  825.5 1.7 copy.55
  827.3 1.3 gather_fusion.3
  829.0 45.7 %copy.56 = bf16[9600,16,128]{0,2,1:T(8,128)(2,1)} copy(bf16[9600,16,128]{2,0,1:T(8,128)(2,1)} %all-to-all-done.4) | data formatting | bytes 78643200 | tf_op jit(solution)/shard_map/all_to_all | solution.py:13
  874.7 19.4 %fusion.14 = (f32[224]{0:T(256)S(1)}, f32[224,9600]{1,0:T(8,128)}) fusion(bf16[9600,2048]{0,1:T(8,128)(2,1)} %bitcast.40, f32[2048]{0:T(1024)S(1)} %copy-done.1, f32[224]{0:T(256)S(1)} %add_rsqrt_fusion, bf16[224,2048]{1,0:T(8,128)(2,1)S(1)} %gather_fusion.3, pred[224]{0:T(512)(128)(4,1)S(1)} %get-tuple-element.15), kind=kOutput, calls=%fused_computation.73 | convolution fusion | flops 8812482560 | bytes 48850912 | tf_op jit(solution)/shard_map/dot_general | solution.py:76
  894.0 13.1 %pmax.7 = f32[224]{0:T(256)S(1)} all-reduce(f32[224]{0:T(256)S(1)} %get-tuple-element.26), channel_id=1, replica_groups=mesh['req'=16,'vocab'=8] {'vocab'}, use_global_device_ids=true, to_apply=%region_12.13 | all-reduce | flops 224 | bytes 1792 | tf_op jit(solution)/shard_map/pmax | solution.py:94
  907.2 5.3 fusion
  912.5 12.8 %all-reduce.3 = (f32[224]{0:T(256)S(1)}, f32[224]{0:T(256)S(1)}, f32[224]{0:T(256)S(1)}) all-reduce(f32[224]{0:T(256)S(1)} %get-tuple-element.5, f32[224]{0:T(256)S(1)} %get-tuple-element.19, f32[224]{0:T(256)S(1)} %get-tuple-element.18), channel_id=1, replica_groups=mesh['req'=16,'vocab'=8] {'vocab'}, use_global_device_ids=true, to_apply=%region_10.11 | all-reduce | flops 672 | bytes 5376 | tf_op jit(solution)/shard_map/psum | solution.py:96
  925.9 1.3 scatter_custom_fusion.1
  927.9 9.9 %all-to-all-start.7 = ((f32[4,16,8]{2,0,1:T(4,128)}), f32[4,16,8]{2,0,1:T(4,128)S(1)}, u32[]{:S(2)}, u32[]{:S(2)}) async-start(f32[4,16,8]{2,0,1:T(4,128)} %copy.59), calls=%async_computation.7 | async-start | bytes 65536 | tf_op jit(solution)/shard_map/all_to_all | solution.py:122
  937.8 1.3 scatter_custom_fusion
  939.8 5.6 all-to-all-done.7
  945.4 3.5 all-to-all-start.5
  949.5 6.9 all-to-all-done.5
  957.7 10.7 %all_to_all.151 = f32[16,4,8]{2,1,0:T(4,128)S(1)} all-to-all(f32[16,4,8]{2,1,0:T(4,128)S(1)} %bitcast.51), channel_id=1, replica_groups=mesh['req'=16,'vocab'=8] {'req'}, dimensions={0} | all-to-all | bytes 4096 | tf_op jit(solution)/shard_map/all_to_all | solution.py:127
  968.5 3.5 all-to-all-start.8
  972.7 6.9 all-to-all-done.8
  (59 shorter events, 11.7 us)
Async XLA Ops:
  2.0 14.8 %all-to-all-start = ((s32[4,16,8]{2,0,1:T(4,128)}), s32[4,16,8]{2,0,1:T(4,128)S(1)}, u32[]{:S(2)}, u32[]{:S(2)}) async-start(s32[4,16,8]{2,0,1:T(4,128)} %copy.50), calls=%async_computation | async-start | bytes 65536 | tf_op jit(solution)/shard_map/all_to_all | solution.py:63
  13.7 7.4 copy-start.4
  16.8 33.6 %all-to-all-start.2 = ((bf16[4,128,2048]{2,0,1:T(4,128)(2,1)}), bf16[4,128,2048]{2,0,1:T(4,128)(2,1)S(1)}, u32[]{:S(2)}, u32[]{:S(2)}) async-start(bf16[4,128,2048]{2,0,1:T(4,128)(2,1)} %copy.52), calls=%async_computation.2 | async-start | bytes 4194304 | tf_op jit(solution)/shard_map/all_to_all | solution.py:62
  50.4 11.6 %all-to-all-start.1 = ((s32[16,4,8]{2,1,0:T(4,128)}), s32[16,4,8]{2,1,0:T(4,128)S(1)}, u32[]{:S(2)}, u32[]{:S(2)}) async-start(s32[16,4,8]{2,1,0:T(4,128)} %broadcast_select_fusion.5), calls=%async_computation.1 | async-start | bytes 65536 | tf_op jit(solution)/shard_map/all_to_all | solution.py:69
  62.0 30.1 %copy-start = (bf16[9600,128]{1,0:T(8,128)(2,1)S(1)}, bf16[9600,128]{1,0:T(8,128)(2,1)}, u32[]{:S(2)}) copy-start(bf16[9600,128]{1,0:T(8,128)(2,1)} %param.11) | copy-start | bytes 7372804
  105.1 6.3 copy-start.5
  105.1 7.6 copy-start.2
  105.1 7.8 copy-start.3
  105.1 723.8 %all-to-all-start.4 = ((bf16[9600,16,128]{2,0,1:T(8,128)(2,1)}), bf16[9600,16,128]{2,0,1:T(8,128)(2,1)}, u32[]{:S(2)}, u32[]{:S(2)}) async-start(bf16[9600,16,128]{2,0,1:T(8,128)(2,1)} %tile.2), calls=%async_computation.4 | async-start | bytes 78643200 | tf_op jit(solution)/shard_map/all_to_all | solution.py:13
  828.9 45.7 %copy-start.1 = (f32[2048]{0:T(1024)S(1)}, f32[2048]{0:T(1024)}, u32[]{:S(2)}) copy-start(f32[2048]{0:T(1024)} %param.10) | copy-start | bytes 24580
  927.9 17.5 %all-to-all-start.7 = ((f32[4,16,8]{2,0,1:T(4,128)}), f32[4,16,8]{2,0,1:T(4,128)S(1)}, u32[]{:S(2)}, u32[]{:S(2)}) async-start(f32[4,16,8]{2,0,1:T(4,128)} %copy.59), calls=%async_computation.7 | async-start | bytes 65536 | tf_op jit(solution)/shard_map/all_to_all | solution.py:122
  945.4 11.0 %all-to-all-start.5 = ((f32[4,16,8]{2,0,1:T(4,128)}), f32[4,16,8]{2,0,1:T(4,128)S(1)}, u32[]{:S(2)}, u32[]{:S(2)}) async-start(f32[4,16,8]{2,0,1:T(4,128)} %copy.57), calls=%async_computation.5 | async-start | bytes 65536 | tf_op jit(solution)/shard_map/all_to_all | solution.py:121
  968.5 11.1 %all-to-all-start.8 = ((f32[16,4,8]{2,1,0:T(4,128)}), f32[16,4,8]{2,1,0:T(4,128)S(1)}, u32[]{:S(2)}, u32[]{:S(2)}) async-start(f32[16,4,8]{2,1,0:T(4,128)} %bitcast.25), calls=%async_computation.8 | async-start | bytes 65536 | tf_op jit(solution)/shard_map/all_to_all | solution.py:128
